TPU v7x, 32 devices: a whole 2x2x4 slice. The times are simulated.
32 devices in a mesh: dp: 4 (over x, core), expert: 8 (over z, y).
Axes of the slice: x: 2, y: 2, z: 4, core: 2. Of those that a mesh axis runs over, the one named last changes fastest.
Arguments:
- inputs: bfloat16 [512, 4096], P(('dp', 'expert')), may hold values from -6 to 6
- grad_out: bfloat16 [512, 4096], P(('dp', 'expert')), may hold values from -0.796875 to 0.796875
- labels: int32 [512, 1], P(('dp', 'expert')), may hold values from 0 to 7; in each aligned block of 16 rows (0 to 15, 16 to 31, ...) at most 3 rows name the same one
- w_gate: bfloat16 [4096, 57344], P('dp', 'expert'), may hold values from -0.09375 to 0.09375
- w_up: bfloat16 [4096, 57344], P('dp', 'expert'), may hold values from -0.09375 to 0.09375
- w_down: bfloat16 [57344, 4096], P('expert', 'dp'), may hold values from -0.0625 to 0.0625
Outputs:
- grad_in: bfloat16 [512, 4096], P(('dp', 'expert'))
- grad_gate: bfloat16 [4096, 57344], P('dp', 'expert')
- grad_up: bfloat16 [4096, 57344], P('dp', 'expert')
- grad_down: bfloat16 [57344, 4096], P('expert', 'dp')
Inputs may be any that keep to these rules, and one draw needn't show every extreme that they name: `labels`: among the 16 rows of one device no expert is named by more than 3 rows, a bound that some block reaches.
All inputs are finite; a program needn't handle non-finite values.
Results may differ from a plain program's by a relative error of at most 0.011.
Values may be sent and summed in bfloat16 or wider, within the bound.
No kernel may reach another device: no remote copies, remote signals or barrier semaphores. Data moves between devices by JAX's collectives and lax.ppermute only.
A program may use at most 192 MiB of HBM per device.

v0:
```python
import jax
import jax.numpy as jnp
from jax import lax
from jax.sharding import PartitionSpec as P

EXPERTS = 8


def nonlinear(gate, up, dhid):
    sig = jax.nn.sigmoid(gate)
    act = gate * sig
    hidden = (act * up).astype(jnp.bfloat16)
    d_up = (dhid * act).astype(jnp.bfloat16)
    d_gate = (dhid * up * sig * (1.0 + gate * (1.0 - sig))).astype(jnp.bfloat16)
    return (hidden, d_up, d_gate)


def contract_rows(left, right):
    return lax.dot_general(
        left, right, (((0,), (0,)), ((), ())), preferred_element_type=jnp.float32
    )


def on_device(inputs, grad_out, labels, w_gate, w_up, w_down):
    members = lax.axis_size("expert")
    replicas = lax.axis_size("dp")
    group = members // EXPERTS
    tok_count = inputs.shape[0]
    width = inputs.shape[1]
    capacity = 3 * tok_count // (2 * EXPERTS)
    label_col = labels[:, 0]
    onehot = (label_col[:, None] == jnp.arange(EXPERTS, dtype=jnp.int32)[None, :]).astype(jnp.int32)
    before = jnp.cumsum(onehot, axis=0) - onehot
    rank_in = jnp.sum(before * onehot, axis=1)
    slot_ids = label_col * capacity + rank_in

    def spread(values):
        buffer = jnp.zeros((EXPERTS * capacity, width), jnp.bfloat16).at[slot_ids].set(values)
        return jnp.repeat(buffer.reshape(EXPERTS, 1, capacity, width), group, axis=0)

    recv_in, recv_grad = (
        lax.all_to_all(
            lax.all_to_all(spread(inputs), "dp", split_axis=3, concat_axis=1, tiled=True),
            "expert",
            split_axis=0,
            concat_axis=0,
            tiled=True,
        ),
        lax.all_to_all(
            lax.all_to_all(spread(grad_out), "dp", split_axis=3, concat_axis=1, tiled=True),
            "expert",
            split_axis=0,
            concat_axis=0,
            tiled=True,
        ),
    )
    columns = width // replicas
    rows_in = recv_in.reshape(-1, columns)
    rows_grad = recv_grad.reshape(-1, columns)
    gate_part = jnp.dot(rows_in, w_gate, preferred_element_type=jnp.float32)
    up_part = jnp.dot(rows_in, w_up, preferred_element_type=jnp.float32)
    dhid_part = lax.dot_general(
        rows_grad, w_down, (((1,), (1,)), ((), ())), preferred_element_type=jnp.float32
    )
    gate, up, dhid = lax.psum((gate_part, up_part, dhid_part), "dp")
    hidden, d_up, d_gate = nonlinear(gate, up, dhid)
    d_rows = lax.dot_general(
        d_gate, w_gate, (((1,), (1,)), ((), ())), preferred_element_type=jnp.float32
    )
    d_rows = d_rows + lax.dot_general(
        d_up, w_up, (((1,), (1,)), ((), ())), preferred_element_type=jnp.float32
    )
    back_rows = lax.all_to_all(
        lax.all_to_all(
            d_rows.reshape(members, replicas, capacity, columns).astype(jnp.bfloat16),
            "dp",
            split_axis=1,
            concat_axis=3,
            tiled=True,
        ),
        "expert",
        split_axis=0,
        concat_axis=0,
        tiled=True,
    ).astype(jnp.float32)
    summed = jnp.sum(back_rows.reshape(EXPERTS, group, capacity, width), axis=1)
    grad_in = summed.reshape(EXPERTS * capacity, width)[slot_ids].astype(jnp.bfloat16)
    grad_gate = contract_rows(rows_in, d_gate).astype(jnp.bfloat16)
    grad_up = contract_rows(rows_in, d_up).astype(jnp.bfloat16)
    grad_down = contract_rows(hidden, rows_grad).astype(jnp.bfloat16)
    return (grad_in, grad_gate, grad_up, grad_down)


def solution(mesh):
    return jax.shard_map(
        on_device,
        mesh=mesh,
        in_specs=(
            P(("dp", "expert"), None),
            P(("dp", "expert"), None),
            P(("dp", "expert"), None),
            P("dp", "expert"),
            P("dp", "expert"),
            P("expert", "dp"),
        ),
        out_specs=(
            P(("dp", "expert"), None),
            P("dp", "expert"),
            P("dp", "expert"),
            P("expert", "dp"),
        ),
        check_vma=False,
    )
```

profile of v0, /device:TPU:0, one launch (start us, length us, event | category | flops | bytes accessed | tf_op | source)
XLA Modules:
  0.0 330.5 jit_solution(10850027350697886702)
XLA Ops:
  7.2 0.7 fusion.7
  7.9 0.8 select_reduce_fusion
  8.8 0.7 fusion.8
  9.4 1.2 scatter_custom_fusion.1
  10.7 0.1 reshape_broadcast_in_dim_reshape.7
  10.8 4.6 %copy.38 = bf16[8,1,3,4096]{0,2,1,3:T(4,128)(2,1)} copy(bf16[8,1,3,4096]{3,2,0,1:T(4,128)(2,1)S(1)} %reshape_broadcast_in_dim_reshape.7) | data formatting | bytes 393216 | tf_op jit(solution)/shard_map/reshape;broadcast_in_dim;reshape | solution.py:39
  15.4 5.8 %reshape.60 = bf16[4,2,12288]{2,1,0:T(2,128)(2,1)} reshape(bf16[4096,1,3,8]{3,2,1,0:T(4,128)(2,1)} %bitcast.43) | data formatting | bytes 393216
  21.2 4.2 %all-to-all-start.2 = ((bf16[4,2,12288]{2,1,0:T(2,128)(2,1)}), bf16[4,2,12288]{2,1,0:T(2,128)(2,1)S(1)}, u32[]{:S(2)}, u32[]{:S(2)}) async-start(bf16[4,2,12288]{2,1,0:T(2,128)(2,1)} %reshape.60), calls=%async_computation.2 | async-start | bytes 393216 | tf_op jit(solution)/shard_map/all_to_all | solution.py:43
  25.4 1.2 scatter_custom_fusion
  26.6 0.1 reshape_broadcast_in_dim_reshape.6
  26.8 4.6 %copy.34 = bf16[8,1,3,4096]{0,2,1,3:T(4,128)(2,1)} copy(bf16[8,1,3,4096]{3,2,0,1:T(4,128)(2,1)S(1)} %reshape_broadcast_in_dim_reshape.6) | data formatting | bytes 393216 | tf_op jit(solution)/shard_map/reshape;broadcast_in_dim;reshape | solution.py:39
  31.4 5.8 %reshape.62 = bf16[4,2,12288]{2,1,0:T(2,128)(2,1)} reshape(bf16[4096,1,3,8]{3,2,1,0:T(4,128)(2,1)} %bitcast.44) | data formatting | bytes 393216
  37.2 0.0 all-to-all-done.2
  37.2 3.4 %all-to-all-start = ((bf16[4,2,12288]{2,1,0:T(2,128)(2,1)}), bf16[4,2,12288]{2,1,0:T(2,128)(2,1)S(1)}, u32[]{:S(2)}, u32[]{:S(2)}) async-start(bf16[4,2,12288]{2,1,0:T(2,128)(2,1)} %reshape.62), calls=%async_computation | async-start | bytes 393216 | tf_op jit(solution)/shard_map/all_to_all | solution.py:50
  40.6 4.8 %reshape.61 = bf16[4096,1,3,8]{3,2,1,0:T(4,128)(2,1)} reshape(bf16[4,2,12288]{2,1,0:T(2,128)(2,1)S(1)} %all-to-all-done.2) | data formatting | bytes 393216
  45.4 6.6 %copy.40 = bf16[8,4,3,1024]{3,1,2,0:T(4,128)(2,1)} copy(bf16[8,4,3,1024]{0,2,3,1:T(4,128)(2,1)} %bitcast.45) | data formatting | bytes 393216 | tf_op jit(solution)/shard_map/all_to_all | solution.py:43
  52.0 0.0 all-to-all-done
  52.0 6.5 %all-to-all-start.3 = ((bf16[8,4,3,1024]{3,1,2,0:T(4,128)(2,1)}), bf16[8,4,3,1024]{3,1,2,0:T(4,128)(2,1)S(1)}, u32[]{:S(2)}, u32[]{:S(2)}) async-start(bf16[8,4,3,1024]{3,1,2,0:T(4,128)(2,1)} %copy.40), calls=%async_computation.3 | async-start | bytes 393216 | tf_op jit(solution)/shard_map/all_to_all | solution.py:42
  58.5 4.8 %reshape.63 = bf16[4096,1,3,8]{3,2,1,0:T(4,128)(2,1)} reshape(bf16[4,2,12288]{2,1,0:T(2,128)(2,1)S(1)} %all-to-all-done) | data formatting | bytes 393216
  63.2 6.7 %copy.36 = bf16[8,4,3,1024]{3,1,2,0:T(4,128)(2,1)} copy(bf16[8,4,3,1024]{0,2,3,1:T(4,128)(2,1)} %bitcast.46) | data formatting | bytes 393216 | tf_op jit(solution)/shard_map/all_to_all | solution.py:50
  69.9 0.0 all-to-all-done.3
  69.9 6.0 %all-to-all-start.1 = ((bf16[8,4,3,1024]{3,1,2,0:T(4,128)(2,1)}), bf16[8,4,3,1024]{3,1,2,0:T(4,128)(2,1)S(1)}, u32[]{:S(2)}, u32[]{:S(2)}) async-start(bf16[8,4,3,1024]{3,1,2,0:T(4,128)(2,1)} %copy.36), calls=%async_computation.1 | async-start | bytes 393216 | tf_op jit(solution)/shard_map/all_to_all | solution.py:49
  75.9 0.2 all-reduce.3.cloned.1.call-start
  76.1 0.1 copy.41
  76.2 0.2 reshape.26
  76.4 9.2 %fusion.12 = f32[96,7168]{1,0:T(8,128)} fusion(bf16[96,1024]{1,0:T(8,128)(2,1)S(1)} %reshape.26, bf16[1024,7168]{1,0:T(8,128)(2,1)} %param.9), kind=kOutput, calls=%fused_computation.27 | convolution fusion | flops 1409286144 | bytes 17629184 | tf_op jit(solution)/shard_map/dot_general | solution.py:60
  85.6 9.2 %fusion.11 = f32[96,7168]{1,0:T(8,128)} fusion(bf16[96,1024]{1,0:T(8,128)(2,1)S(1)} %reshape.26, bf16[1024,7168]{1,0:T(8,128)(2,1)} %param.10), kind=kOutput, calls=%fused_computation.26 | convolution fusion | flops 1409286144 | bytes 17629184 | tf_op jit(solution)/shard_map/dot_general | solution.py:61
  94.7 0.0 all-to-all-done.1
  94.7 0.1 copy.37
  94.9 0.2 reshape.25
  95.0 11.3 %fusion.10 = f32[96,7168]{1,0:T(8,128)} fusion(bf16[96,1024]{1,0:T(8,128)(2,1)S(1)} %reshape.25, bf16[7168,1024]{1,0:T(8,128)(2,1)} %param.11), kind=kOutput, calls=%fused_computation.25 | convolution fusion | flops 1409286144 | bytes 17629184 | tf_op jit(solution)/shard_map/dot_general | solution.py:62
  106.3 0.0 all-reduce.3.cloned.1.call-update
  106.4 153.3 %all-reduce.3.cloned.1.call-done = (f32[96,7168]{1,0:T(8,128)}, f32[96,7168]{1,0:T(8,128)}, f32[96,7168]{1,0:T(8,128)}) async-done(((f32[96,7168]{1,0:T(8,128)}, f32[96,7168]{1,0:T(8,128)}, f32[96,7168]{1,0:T(8,128)}), (f32[96,7168]{1,0:T(8,128)}, f32[96,7168]{1,0:T(8,128)}, f32[96,7168]{1,0:T(8,128)})) %all-reduce.3.cloned.1.call-update) | async-done | bytes 8257552 | tf_op jit(solution)/shard_map/psum | solution.py:65
  259.6 0.0 copy-start
  259.6 10.3 %convolution_convert_fusion = bf16[7168,1024]{1,0:T(8,128)(2,1)} fusion(bf16[96,1024]{1,0:T(8,128)(2,1)S(1)} %reshape.25, f32[96,7168]{1,0:T(8,128)} %get-tuple-element.6, f32[96,7168]{1,0:T(8,128)} %get-tuple-element.4), kind=kOutput, calls=%fused_computation.3 | convolution fusion | flops 1420754944 | bytes 20381696 | tf_op jit(solution)/shard_map/dot_general | solution.py:19
  270.0 0.0 copy-done
  270.0 4.0 %multiply_convert_fusion.1 = (bf16[96,7168]{1,0:T(8,128)(2,1)S(1)}, bf16[96,7168]{1,0:T(8,128)(2,1)S(1)}) fusion(f32[96,7168]{1,0:T(8,128)} %get-tuple-element.5, f32[96,7168]{1,0:T(8,128)S(1)} %copy-done, f32[96,7168]{1,0:T(8,128)} %get-tuple-element.6), kind=kLoop, calls=%fused_computation.7 | loop fusion | flops 8945664 | bytes 11010048 | tf_op jit(solution)/shard_map/convert_element_type | solution.py:13
  274.0 0.0 copy-start.1
  274.0 10.3 %fusion.13 = f32[96,1024]{1,0:T(8,128)S(1)} fusion(bf16[96,7168]{1,0:T(8,128)(2,1)S(1)} %get-tuple-element.8, bf16[1024,7168]{1,0:T(8,128)(2,1)} %param.9), kind=kOutput, calls=%fused_computation.28 | convolution fusion | flops 1409286144 | bytes 16449536 | tf_op jit(solution)/shard_map/dot_general | solution.py:67
  284.2 0.0 copy-done.1
  284.3 9.9 %fusion.1 = bf16[96,1024]{1,0:T(8,128)(2,1)S(1)} fusion(f32[96,1024]{1,0:T(8,128)S(1)} %fusion.13, bf16[96,7168]{1,0:T(8,128)(2,1)S(1)} %get-tuple-element.7, bf16[1024,7168]{1,0:T(8,128)(2,1)} %param.10), kind=kOutput, calls=%fused_computation.12 | convolution fusion | flops 1409482752 | bytes 16646144 | tf_op jit(solution)/shard_map/dot_general | solution.py:70
  294.2 0.1 convert_element_type.35
  294.3 0.8 copy.42
  295.1 3.6 %all-to-all-start.4 = ((bf16[8,4,3,1024]{3,0,2,1:T(8,128)(2,1)}), bf16[8,4,3,1024]{3,0,2,1:T(8,128)(2,1)S(1)}, u32[]{:S(2)}, u32[]{:S(2)}) async-start(bf16[8,4,3,1024]{3,0,2,1:T(8,128)(2,1)} %copy.42), calls=%async_computation.4 | async-start | bytes 393216 | tf_op jit(solution)/shard_map/all_to_all | solution.py:74
  298.8 7.6 %convolution_convert_fusion.1 = bf16[1024,7168]{1,0:T(8,128)(2,1)} fusion(bf16[96,1024]{1,0:T(8,128)(2,1)S(1)} %reshape.26, bf16[96,7168]{1,0:T(8,128)(2,1)S(1)} %get-tuple-element.7), kind=kOutput, calls=%fused_computation.4 | convolution fusion | flops 1416626176 | bytes 16252928 | tf_op jit(solution)/shard_map/dot_general | solution.py:19
  306.4 0.0 all-to-all-done.4
  306.4 0.2 copy.49
  306.5 0.9 reshape.55
  307.4 5.5 %all-to-all-start.5 = ((bf16[8,1,3,4096]{3,2,1,0:T(4,128)(2,1)}), bf16[8,1,3,4096]{3,2,1,0:T(4,128)(2,1)S(1)}, u32[]{:S(2)}, u32[]{:S(2)}) async-start(bf16[8,1,3,4096]{3,2,1,0:T(4,128)(2,1)} %reshape.55), calls=%async_computation.5 | async-start | bytes 524288 | tf_op jit(solution)/shard_map/all_to_all | solution.py:73
  312.9 8.9 %convolution_convert_fusion.2 = bf16[1024,7168]{1,0:T(8,128)(2,1)} fusion(bf16[96,1024]{1,0:T(8,128)(2,1)S(1)} %reshape.26, bf16[96,7168]{1,0:T(8,128)(2,1)} %copy-done.1), kind=kOutput, calls=%fused_computation.5 | convolution fusion | flops 1416626176 | bytes 16252928 | tf_op jit(solution)/shard_map/dot_general | solution.py:19
  321.8 0.3 all-to-all-done.5
  322.2 0.2 reshape.30
  322.3 1.3 gather_fusion
  (2 shorter events, 0.0 us)
Async XLA Ops:
  21.2 16.0 %all-to-all-start.2 = ((bf16[4,2,12288]{2,1,0:T(2,128)(2,1)}), bf16[4,2,12288]{2,1,0:T(2,128)(2,1)S(1)}, u32[]{:S(2)}, u32[]{:S(2)}) async-start(bf16[4,2,12288]{2,1,0:T(2,128)(2,1)} %reshape.60), calls=%async_computation.2 | async-start | bytes 393216 | tf_op jit(solution)/shard_map/all_to_all | solution.py:43
  37.2 14.8 %all-to-all-start = ((bf16[4,2,12288]{2,1,0:T(2,128)(2,1)}), bf16[4,2,12288]{2,1,0:T(2,128)(2,1)S(1)}, u32[]{:S(2)}, u32[]{:S(2)}) async-start(bf16[4,2,12288]{2,1,0:T(2,128)(2,1)} %reshape.62), calls=%async_computation | async-start | bytes 393216 | tf_op jit(solution)/shard_map/all_to_all | solution.py:50
  52.0 17.9 %all-to-all-start.3 = ((bf16[8,4,3,1024]{3,1,2,0:T(4,128)(2,1)}), bf16[8,4,3,1024]{3,1,2,0:T(4,128)(2,1)S(1)}, u32[]{:S(2)}, u32[]{:S(2)}) async-start(bf16[8,4,3,1024]{3,1,2,0:T(4,128)(2,1)} %copy.40), calls=%async_computation.3 | async-start | bytes 393216 | tf_op jit(solution)/shard_map/all_to_all | solution.py:42
  69.9 24.8 %all-to-all-start.1 = ((bf16[8,4,3,1024]{3,1,2,0:T(4,128)(2,1)}), bf16[8,4,3,1024]{3,1,2,0:T(4,128)(2,1)S(1)}, u32[]{:S(2)}, u32[]{:S(2)}) async-start(bf16[8,4,3,1024]{3,1,2,0:T(4,128)(2,1)} %copy.36), calls=%async_computation.1 | async-start | bytes 393216 | tf_op jit(solution)/shard_map/all_to_all | solution.py:49
  75.9 183.8 %all-reduce.3.cloned.1.call-start = ((), (), s32[]{:S(2)}) async-start(), calls=%async_computation.6 | async-start | bytes 16515072 | tf_op jit(solution)/shard_map/psum | solution.py:65
  259.6 10.3 %copy-start = (f32[96,7168]{1,0:T(8,128)S(1)}, f32[96,7168]{1,0:T(8,128)}, u32[]{:S(2)}) copy-start(f32[96,7168]{1,0:T(8,128)} %get-tuple-element.4) | copy-start | bytes 8257540
  274.0 10.3 %copy-start.1 = (bf16[96,7168]{1,0:T(8,128)(2,1)}, bf16[96,7168]{1,0:T(8,128)(2,1)S(1)}, u32[]{:S(2)}) copy-start(bf16[96,7168]{1,0:T(8,128)(2,1)S(1)} %get-tuple-element.8) | copy-start | bytes 4128772
  295.1 11.2 %all-to-all-start.4 = ((bf16[8,4,3,1024]{3,0,2,1:T(8,128)(2,1)}), bf16[8,4,3,1024]{3,0,2,1:T(8,128)(2,1)S(1)}, u32[]{:S(2)}, u32[]{:S(2)}) async-start(bf16[8,4,3,1024]{3,0,2,1:T(8,128)(2,1)} %copy.42), calls=%async_computation.4 | async-start | bytes 393216 | tf_op jit(solution)/shard_map/all_to_all | solution.py:74
  307.4 14.8 %all-to-all-start.5 = ((bf16[8,1,3,4096]{3,2,1,0:T(4,128)(2,1)}), bf16[8,1,3,4096]{3,2,1,0:T(4,128)(2,1)S(1)}, u32[]{:S(2)}, u32[]{:S(2)}) async-start(bf16[8,1,3,4096]{3,2,1,0:T(4,128)(2,1)} %reshape.55), calls=%async_computation.5 | async-start | bytes 524288 | tf_op jit(solution)/shard_map/all_to_all | solution.py:73
Sparse Core Ops, SparseCore 0:
  106.5 153.1 all-reduce.2
where the time goes:
time: 332 us; the launch traced here: 330 us
  waiting for transfers between devices  154 us (46%)
  matrix products  76.6 us (23%)
  local copies, waits for them, and re-layouts  50.4 us (15%)
  starting transfers between devices  29.4 us (9%)
  between operations  14.2 us (4%)
  other arithmetic  6.24 us (2%)
    psum x1, waiting for transfers between devices, on_device(): gate, up, dhid = lax.psum((gate_part, up_part, dhid_part), 'dp')  153 us
    dot_general x3, matrix products, contract_rows(): lax.dot_general(left, right, (((0,), (0,)), ((), ())), preferred_element_...  26.9 us
    unnamed x8, local copies, waits for them, and re-layouts  21.2 us
    dot_general x1, matrix products, on_device(): lax.dot_general(rows_grad, w_down, (((1,), (1,)), ((), ())), preferred_el...  11.3 us
    dot_general x1, matrix products, on_device(): lax.dot_general(d_gate, w_gate, (((1,), (1,)), ((), ())), preferred_eleme...  10.3 us
    dot_general x1, matrix products, on_device(): lax.dot_general(d_up, w_up, (((1,), (1,)), ((), ())), preferred_element_t...  9.9 us
    another operation x4, local copies, waits for them, and re-layouts, spread(): jnp.repeat(buffer.reshape(EXPERTS, 1, capacity, width), group, axis=0)  9.43 us
    dot_general x1, matrix products, on_device(): gate_part = jnp.dot(rows_in, w_gate, preferred_element_type=jnp.float32)  9.16 us
  transfers between devices with their start and end apart: 7, of which 2 were waited for; matrix products, arithmetic and copies ran while one was open for 21% of the time, Pallas kernels for 0%

commit v1 on v0

--- a/solution.py
+++ b/solution.py
@@ -4,6 +4,22 @@
 from jax.sharding import PartitionSpec as P
 
 EXPERTS = 8
+
+
+def pairwise_exchange(value, axis, split, join):
+    ways, here = (lax.axis_size(axis), lax.axis_index(axis))
+    width = value.shape[split] // ways
+    lengths = list(value.shape)
+    lengths[split] = width
+    height = lengths[join]
+    lengths[join] = height * ways
+    full = jnp.zeros(lengths, value.dtype)
+    for mask in range(ways):
+        part = lax.dynamic_slice_in_dim(value, (here ^ mask) * width, width, axis=split)
+        if mask:
+            part = lax.ppermute(part, axis, [(d, d ^ mask) for d in range(ways)])
+        full = lax.dynamic_update_slice_in_dim(full, part, (here ^ mask) * height, axis=join)
+    return full
 
 
 def nonlinear(gate, up, dhid):
@@ -47,7 +63,7 @@
             tiled=True,
         ),
         lax.all_to_all(
-            lax.all_to_all(spread(grad_out), "dp", split_axis=3, concat_axis=1, tiled=True),
+            pairwise_exchange(spread(grad_out), "dp", 3, 1),
             "expert",
             split_axis=0,
             concat_axis=0,

time: 332 us -> 321 us (0.967)
  local copies, waits for them, and re-layouts: 50.4 us -> 40.7 us
    dynamic_update_slice x0 -> x4, local copies, waits for them, and re-layouts: none -> 10.9 us  [pairwise_exchange(): lax.dynamic_update_slice_in_dim(full, part, (here ^ mask) * height, axis=...]
    unnamed x8 -> x6, local copies, waits for them, and re-layouts: 21.2 us -> 10.6 us
    all_to_all x2 -> x1, local copies, waits for them, and re-layouts: 6.79 us -> 0.14 us  [on_device(): lax.all_to_all(pairwise_exchange(spread(grad_out), 'dp', 3, 1), 'expert',...]
    another operation x4 -> x3, local copies, waits for them, and re-layouts: 9.43 us -> 4.84 us  [spread(): jnp.repeat(buffer.reshape(EXPERTS, 1, capacity, width), group, axis=0)]
    all_to_all x2 -> x1, starting transfers between devices: 9.35 us -> 6.34 us  [on_device(): lax.all_to_all(pairwise_exchange(spread(grad_out), 'dp', 3, 1), 'expert',...]
  transfers between devices with their start and end apart: 7 -> 9, of which waited for: 2 -> 2; matrix products, arithmetic and copies ran while one was open for 21% -> 17% of each run, Pallas kernels for 0% -> 0%
where the time goes in v1:
time: 321 us; the launch traced here: 319 us
  waiting for transfers between devices  153 us (48%)
  matrix products  76.6 us (24%)
  local copies, waits for them, and re-layouts  40.7 us (13%)
  starting transfers between devices  28.2 us (9%)
  between operations  14.2 us (4%)
  other arithmetic  6.24 us (2%)
    psum x1, waiting for transfers between devices, on_device(): gate, up, dhid = lax.psum((gate_part, up_part, dhid_part), 'dp')  153 us
    dot_general x3, matrix products, contract_rows(): lax.dot_general(left, right, (((0,), (0,)), ((), ())), preferred_element_...  26.9 us
    dot_general x1, matrix products, on_device(): lax.dot_general(rows_grad, w_down, (((1,), (1,)), ((), ())), preferred_el...  11.3 us
    dynamic_update_slice x4, local copies, waits for them, and re-layouts, pairwise_exchange(): lax.dynamic_update_slice_in_dim(full, part, (here ^ mask) * height, axis=...  10.9 us
    unnamed x6, local copies, waits for them, and re-layouts  10.6 us
    dot_general x1, matrix products, on_device(): lax.dot_general(d_gate, w_gate, (((1,), (1,)), ((), ())), preferred_eleme...  10.3 us
    dot_general x1, matrix products, on_device(): lax.dot_general(d_up, w_up, (((1,), (1,)), ((), ())), preferred_element_t...  9.9 us
    dot_general x1, matrix products, on_device(): gate_part = jnp.dot(rows_in, w_gate, preferred_element_type=jnp.float32)  9.16 us
  transfers between devices with their start and end apart: 9, of which 2 were waited for; matrix products, arithmetic and copies ran while one was open for 17% of the time, Pallas kernels for 0%

profile of v1, /device:TPU:0, one launch (start us, length us, event | category | flops | bytes accessed | tf_op | source)
XLA Modules:
  0.0 319.3 jit_solution(5754761123755076392)
XLA Ops:
  7.2 0.7 fusion.7
  7.9 0.8 select_reduce_fusion
  8.8 0.7 fusion.8
  9.4 1.2 scatter_custom_fusion.1
  10.7 0.1 reshape_broadcast_in_dim_reshape.7
  10.8 4.6 %copy.43 = bf16[8,1,3,4096]{0,2,1,3:T(4,128)(2,1)} copy(bf16[8,1,3,4096]{3,2,0,1:T(4,128)(2,1)S(1)} %reshape_broadcast_in_dim_reshape.7) | data formatting | bytes 393216 | tf_op jit(solution)/shard_map/reshape;broadcast_in_dim;reshape | solution.py:55
  15.4 5.8 %reshape.60 = bf16[4,2,12288]{2,1,0:T(2,128)(2,1)} reshape(bf16[4096,1,3,8]{3,2,1,0:T(4,128)(2,1)} %bitcast.36) | data formatting | bytes 393216
  21.2 4.2 %all-to-all-start.1 = ((bf16[4,2,12288]{2,1,0:T(2,128)(2,1)}), bf16[4,2,12288]{2,1,0:T(2,128)(2,1)S(1)}, u32[]{:S(2)}, u32[]{:S(2)}) async-start(bf16[4,2,12288]{2,1,0:T(2,128)(2,1)} %reshape.60), calls=%async_computation.1 | async-start | bytes 393216 | tf_op jit(solution)/shard_map/all_to_all | solution.py:59
  25.4 1.2 scatter_custom_fusion
  26.6 0.1 reshape_broadcast_in_dim_reshape.6
  26.8 0.1 constant_dynamic-slice_fusion
  26.9 0.6 collective-permute-start
  27.5 1.7 collective-permute-start.1
  29.2 0.1 collective-permute-start.2
  29.2 0.1 copy.38
  29.3 0.7 broadcast_in_dim.2
  30.1 2.7 dynamic_update_slice.12
  32.8 0.0 collective-permute-done
  32.8 0.1 copy.39
  32.9 2.7 dynamic_update_slice.13
  35.6 0.0 collective-permute-done.1
  35.6 0.1 copy.40
  35.7 2.7 dynamic_update_slice.14
  38.4 0.0 collective-permute-done.2
  38.4 0.1 copy.41
  38.5 2.7 dynamic_update_slice.15
  41.3 0.0 all-to-all-done.1
  41.3 6.3 %all-to-all-start = ((bf16[8,4,3,1024]{3,1,2,0:T(4,128)(2,1)}), bf16[8,4,3,1024]{3,1,2,0:T(4,128)(2,1)S(1)}, u32[]{:S(2)}, u32[]{:S(2)}) async-start(bf16[8,4,3,1024]{3,1,2,0:T(4,128)(2,1)} %dynamic_update_slice.15), calls=%async_computation | async-start | bytes 393216 | tf_op jit(solution)/shard_map/all_to_all | solution.py:65
  47.6 4.8 %reshape.61 = bf16[4096,1,3,8]{3,2,1,0:T(4,128)(2,1)} reshape(bf16[4,2,12288]{2,1,0:T(2,128)(2,1)S(1)} %all-to-all-done.1) | data formatting | bytes 393216
  52.4 6.6 %copy.45 = bf16[8,4,3,1024]{3,1,2,0:T(4,128)(2,1)} copy(bf16[8,4,3,1024]{0,2,3,1:T(4,128)(2,1)} %bitcast.37) | data formatting | bytes 393216 | tf_op jit(solution)/shard_map/all_to_all | solution.py:59
  59.0 0.0 all-to-all-done
  59.0 6.0 %all-to-all-start.2 = ((bf16[8,4,3,1024]{3,1,2,0:T(4,128)(2,1)}), bf16[8,4,3,1024]{3,1,2,0:T(4,128)(2,1)S(1)}, u32[]{:S(2)}, u32[]{:S(2)}) async-start(bf16[8,4,3,1024]{3,1,2,0:T(4,128)(2,1)} %copy.45), calls=%async_computation.2 | async-start | bytes 393216 | tf_op jit(solution)/shard_map/all_to_all | solution.py:58
  65.0 0.2 all-reduce.3.cloned.1.call-start
  65.2 0.1 copy.42
  65.4 0.2 reshape.25
  65.6 11.3 %fusion.10 = f32[96,7168]{1,0:T(8,128)} fusion(bf16[96,1024]{1,0:T(8,128)(2,1)S(1)} %reshape.25, bf16[7168,1024]{1,0:T(8,128)(2,1)} %param.11), kind=kOutput, calls=%fused_computation.29 | convolution fusion | flops 1409286144 | bytes 17629184 | tf_op jit(solution)/shard_map/dot_general | solution.py:78
  76.8 0.0 all-to-all-done.2
  76.8 0.1 copy.46
  77.0 0.2 reshape.26
  77.2 9.2 %fusion.12 = f32[96,7168]{1,0:T(8,128)} fusion(bf16[96,1024]{1,0:T(8,128)(2,1)S(1)} %reshape.26, bf16[1024,7168]{1,0:T(8,128)(2,1)} %param.9), kind=kOutput, calls=%fused_computation.31 | convolution fusion | flops 1409286144 | bytes 17629184 | tf_op jit(solution)/shard_map/dot_general | solution.py:76
  86.3 9.2 %fusion.11 = f32[96,7168]{1,0:T(8,128)} fusion(bf16[96,1024]{1,0:T(8,128)(2,1)S(1)} %reshape.26, bf16[1024,7168]{1,0:T(8,128)(2,1)} %param.10), kind=kOutput, calls=%fused_computation.30 | convolution fusion | flops 1409286144 | bytes 17629184 | tf_op jit(solution)/shard_map/dot_general | solution.py:77
  95.5 0.0 all-reduce.3.cloned.1.call-update
  95.5 153.0 %all-reduce.3.cloned.1.call-done = (f32[96,7168]{1,0:T(8,128)}, f32[96,7168]{1,0:T(8,128)}, f32[96,7168]{1,0:T(8,128)}) async-done(((f32[96,7168]{1,0:T(8,128)}, f32[96,7168]{1,0:T(8,128)}, f32[96,7168]{1,0:T(8,128)}), (f32[96,7168]{1,0:T(8,128)}, f32[96,7168]{1,0:T(8,128)}, f32[96,7168]{1,0:T(8,128)})) %all-reduce.3.cloned.1.call-update) | async-done | bytes 8257552 | tf_op jit(solution)/shard_map/psum | solution.py:81
  248.5 0.0 copy-start
  248.5 10.3 %convolution_convert_fusion = bf16[7168,1024]{1,0:T(8,128)(2,1)} fusion(bf16[96,1024]{1,0:T(8,128)(2,1)S(1)} %reshape.25, f32[96,7168]{1,0:T(8,128)} %get-tuple-element.6, f32[96,7168]{1,0:T(8,128)} %get-tuple-element.4), kind=kOutput, calls=%fused_computation.3 | convolution fusion | flops 1420754944 | bytes 20381696 | tf_op jit(solution)/shard_map/dot_general | solution.py:35
  258.9 0.0 copy-done
  258.9 4.0 %multiply_convert_fusion.1 = (bf16[96,7168]{1,0:T(8,128)(2,1)S(1)}, bf16[96,7168]{1,0:T(8,128)(2,1)S(1)}) fusion(f32[96,7168]{1,0:T(8,128)} %get-tuple-element.5, f32[96,7168]{1,0:T(8,128)S(1)} %copy-done, f32[96,7168]{1,0:T(8,128)} %get-tuple-element.6), kind=kLoop, calls=%fused_computation.7 | loop fusion | flops 8945664 | bytes 11010048 | tf_op jit(solution)/shard_map/convert_element_type | solution.py:29
  262.8 0.0 copy-start.1
  262.8 10.3 %fusion.13 = f32[96,1024]{1,0:T(8,128)S(1)} fusion(bf16[96,7168]{1,0:T(8,128)(2,1)S(1)} %get-tuple-element.8, bf16[1024,7168]{1,0:T(8,128)(2,1)} %param.9), kind=kOutput, calls=%fused_computation.32 | convolution fusion | flops 1409286144 | bytes 16449536 | tf_op jit(solution)/shard_map/dot_general | solution.py:83
  273.1 0.0 copy-done.1
  273.1 9.9 %fusion.1 = bf16[96,1024]{1,0:T(8,128)(2,1)S(1)} fusion(f32[96,1024]{1,0:T(8,128)S(1)} %fusion.13, bf16[96,7168]{1,0:T(8,128)(2,1)S(1)} %get-tuple-element.7, bf16[1024,7168]{1,0:T(8,128)(2,1)} %param.10), kind=kOutput, calls=%fused_computation.12 | convolution fusion | flops 1409482752 | bytes 16646144 | tf_op jit(solution)/shard_map/dot_general | solution.py:86
  283.0 0.1 convert_element_type.35
  283.2 0.8 copy.47
  284.0 3.6 %all-to-all-start.3 = ((bf16[8,4,3,1024]{3,0,2,1:T(8,128)(2,1)}), bf16[8,4,3,1024]{3,0,2,1:T(8,128)(2,1)S(1)}, u32[]{:S(2)}, u32[]{:S(2)}) async-start(bf16[8,4,3,1024]{3,0,2,1:T(8,128)(2,1)} %copy.47), calls=%async_computation.3 | async-start | bytes 393216 | tf_op jit(solution)/shard_map/all_to_all | solution.py:90
  287.6 7.6 %convolution_convert_fusion.1 = bf16[1024,7168]{1,0:T(8,128)(2,1)} fusion(bf16[96,1024]{1,0:T(8,128)(2,1)S(1)} %reshape.26, bf16[96,7168]{1,0:T(8,128)(2,1)S(1)} %get-tuple-element.7), kind=kOutput, calls=%fused_computation.4 | convolution fusion | flops 1416626176 | bytes 16252928 | tf_op jit(solution)/shard_map/dot_general | solution.py:35
  295.2 0.0 all-to-all-done.3
  295.2 0.2 copy.52
  295.4 0.9 reshape.55
  296.2 5.5 %all-to-all-start.4 = ((bf16[8,1,3,4096]{3,2,1,0:T(4,128)(2,1)}), bf16[8,1,3,4096]{3,2,1,0:T(4,128)(2,1)S(1)}, u32[]{:S(2)}, u32[]{:S(2)}) async-start(bf16[8,1,3,4096]{3,2,1,0:T(4,128)(2,1)} %reshape.55), calls=%async_computation.4 | async-start | bytes 524288 | tf_op jit(solution)/shard_map/all_to_all | solution.py:89
  301.8 8.9 %convolution_convert_fusion.2 = bf16[1024,7168]{1,0:T(8,128)(2,1)} fusion(bf16[96,1024]{1,0:T(8,128)(2,1)S(1)} %reshape.26, bf16[96,7168]{1,0:T(8,128)(2,1)} %copy-done.1), kind=kOutput, calls=%fused_computation.5 | convolution fusion | flops 1416626176 | bytes 16252928 | tf_op jit(solution)/shard_map/dot_general | solution.py:35
  310.7 0.4 all-to-all-done.4
  311.0 0.2 reshape.30
  311.2 1.3 gather_fusion
  (2 shorter events, 0.0 us)
Async XLA Ops:
  21.2 20.1 %all-to-all-start.1 = ((bf16[4,2,12288]{2,1,0:T(2,128)(2,1)}), bf16[4,2,12288]{2,1,0:T(2,128)(2,1)S(1)}, u32[]{:S(2)}, u32[]{:S(2)}) async-start(bf16[4,2,12288]{2,1,0:T(2,128)(2,1)} %reshape.60), calls=%async_computation.1 | async-start | bytes 393216 | tf_op jit(solution)/shard_map/all_to_all | solution.py:59
  26.9 5.9 %collective-permute-start = (bf16[8,1,3,1024]{3,2,0,1:T(4,128)(2,1)S(1)}, bf16[8,1,3,1024]{3,2,0,1:T(4,128)(2,1)S(1)}, u32[]{:S(2)}, u32[]{:S(2)}) collective-permute-start(bf16[8,1,3,1024]{3,2,0,1:T(4,128)(2,1)S(1)} %get-tuple-element.11), channel_id=1, source_target_pairs={{0,8},{8,0},{16,24},{24,16},{1,9},{9,1},{17,25},{25,17},{2,10},{10... | collective-permute-start | bytes 147464 | tf_op jit(solution)/shard_map/ppermute | solution.py:20
  27.5 8.1 %collective-permute-start.1 = (bf16[8,1,3,1024]{3,2,0,1:T(4,128)(2,1)S(1)}, bf16[8,1,3,1024]{3,2,0,1:T(4,128)(2,1)S(1)}, u32[]{:S(2)}, u32[]{:S(2)}) collective-permute-start(bf16[8,1,3,1024]{3,2,0,1:T(4,128)(2,1)S(1)} %get-tuple-element.10), channel_id=1, source_target_pairs={{0,16},{8,24},{16,0},{24,8},{1,17},{9,25},{17,1},{25,9},{2,18},{10... | collective-permute-start | bytes 147464 | tf_op jit(solution)/shard_map/ppermute | solution.py:20
  29.2 9.3 %collective-permute-start.2 = (bf16[8,1,3,1024]{3,2,0,1:T(4,128)(2,1)S(1)}, bf16[8,1,3,1024]{3,2,0,1:T(4,128)(2,1)S(1)}, u32[]{:S(2)}, u32[]{:S(2)}) collective-permute-start(bf16[8,1,3,1024]{3,2,0,1:T(4,128)(2,1)S(1)} %get-tuple-element.9), channel_id=1, source_target_pairs={{0,24},{8,16},{16,8},{24,0},{1,25},{9,17},{17,9},{25,1},{2,26},{10... | collective-permute-start | bytes 147464 | tf_op jit(solution)/shard_map/ppermute | solution.py:20
  41.3 17.8 %all-to-all-start = ((bf16[8,4,3,1024]{3,1,2,0:T(4,128)(2,1)}), bf16[8,4,3,1024]{3,1,2,0:T(4,128)(2,1)S(1)}, u32[]{:S(2)}, u32[]{:S(2)}) async-start(bf16[8,4,3,1024]{3,1,2,0:T(4,128)(2,1)} %dynamic_update_slice.15), calls=%async_computation | async-start | bytes 393216 | tf_op jit(solution)/shard_map/all_to_all | solution.py:65
  59.0 17.8 %all-to-all-start.2 = ((bf16[8,4,3,1024]{3,1,2,0:T(4,128)(2,1)}), bf16[8,4,3,1024]{3,1,2,0:T(4,128)(2,1)S(1)}, u32[]{:S(2)}, u32[]{:S(2)}) async-start(bf16[8,4,3,1024]{3,1,2,0:T(4,128)(2,1)} %copy.45), calls=%async_computation.2 | async-start | bytes 393216 | tf_op jit(solution)/shard_map/all_to_all | solution.py:58
  65.0 183.5 %all-reduce.3.cloned.1.call-start = ((), (), s32[]{:S(2)}) async-start(), calls=%async_computation.5 | async-start | bytes 16515072 | tf_op jit(solution)/shard_map/psum | solution.py:81
  248.5 10.4 %copy-start = (f32[96,7168]{1,0:T(8,128)S(1)}, f32[96,7168]{1,0:T(8,128)}, u32[]{:S(2)}) copy-start(f32[96,7168]{1,0:T(8,128)} %get-tuple-element.4) | copy-start | bytes 8257540
  262.8 10.3 %copy-start.1 = (bf16[96,7168]{1,0:T(8,128)(2,1)}, bf16[96,7168]{1,0:T(8,128)(2,1)S(1)}, u32[]{:S(2)}) copy-start(bf16[96,7168]{1,0:T(8,128)(2,1)S(1)} %get-tuple-element.8) | copy-start | bytes 4128772
  284.0 11.2 %all-to-all-start.3 = ((bf16[8,4,3,1024]{3,0,2,1:T(8,128)(2,1)}), bf16[8,4,3,1024]{3,0,2,1:T(8,128)(2,1)S(1)}, u32[]{:S(2)}, u32[]{:S(2)}) async-start(bf16[8,4,3,1024]{3,0,2,1:T(8,128)(2,1)} %copy.47), calls=%async_computation.3 | async-start | bytes 393216 | tf_op jit(solution)/shard_map/all_to_all | solution.py:90
  296.2 14.8 %all-to-all-start.4 = ((bf16[8,1,3,4096]{3,2,1,0:T(4,128)(2,1)}), bf16[8,1,3,4096]{3,2,1,0:T(4,128)(2,1)S(1)}, u32[]{:S(2)}, u32[]{:S(2)}) async-start(bf16[8,1,3,4096]{3,2,1,0:T(4,128)(2,1)} %reshape.55), calls=%async_computation.4 | async-start | bytes 524288 | tf_op jit(solution)/shard_map/all_to_all | solution.py:89
Sparse Core Ops, SparseCore 0:
  95.6 152.8 all-reduce.2
